TPU v7x, 256 devices: a whole 4x4x8 slice. The times are simulated.
256 devices in a mesh: seq: 64 (over x, z, core), mp: 4 (over y).
Axes of the slice: x: 4, y: 4, z: 8, core: 2. Of those that a mesh axis runs over, the one named last changes fastest.
Arguments:
- states: bfloat16 [4, 128, 2560], P(None, 'seq', 'mp'), may hold values from -6 to 6
- norm_gain: float32 [2560], replicated, may hold values from 0.5 to 2
- query_gain: float32 [128], replicated, may hold values from 0.7 to 2
- key_gain: float32 [128], replicated, may hold values from 0.7 to 2
- w_query: bfloat16 [2560, 2048], P(None, 'mp'), may hold values from -0.125 to 0.125
- key_matrix: bfloat16 [2560, 512], P(None, 'mp'), may hold values from -0.125 to 0.125
- value_matrix: bfloat16 [2560, 512], P(None, 'mp'), may hold values from -0.125 to 0.125
- w_out: bfloat16 [2048, 2560], P('mp'), may hold values from -0.125 to 0.125
- cached_key_blocks: bfloat16 [1024, 256, 512], P('seq', None, 'mp'), may hold values from -216 to 216
- cached_value_blocks: bfloat16 [1024, 256, 512], P('seq', None, 'mp'), may hold values from -6 to 6
- req_len: int32 [128], replicated, may hold values from 1 to 16384, as said below
- slot_request: int32 [1024], P('seq'), may hold values from 0 to 127, as said below
- slot_block: int32 [1024], P('seq'), may hold values from 0 to 63
- slot_empty: int32 [1024], P('seq'), may hold values from 0 to 1
Outputs:
- hidden: bfloat16 [4, 128, 2560], P(None, 'seq', 'mp')
- new_keys: bfloat16 [4, 128, 512], P(None, 'seq', 'mp')
- new_values: bfloat16 [4, 128, 512], P(None, 'seq', 'mp')
Inputs may be any that keep to these rules, and one draw needn't show every extreme that they name: `req_len`: exactly 12 requests have length 16384; each other request has length at most 511, and one of them exactly that. Slot s holds positions slot_block[s] * 256 onward of request slot_request[s] unless slot_empty[s] = 1. Each block of a request below its length lies in exactly one slot that is not empty. A request of length 16384 has one block on every index of seq; every block of any other request b lies on index b // 2 of seq.
All inputs are finite; a program needn't handle non-finite values.
Results may differ from a plain program's by a relative error of at most 0.0098.
Values may be sent and summed in bfloat16 or wider, within the bound.
No kernel may reach another device: no remote copies, remote signals or barrier semaphores. Data moves between devices by JAX's collectives and lax.ppermute only.
A program may use at most 64 MiB of HBM per device.

v0:
```python
import jax
import jax.numpy as jnp
from jax import lax
from jax.sharding import PartitionSpec as P

HEAD_SIZE = 128
STEPS = 4
ROPE_BASE = 1000000.0
NEGATIVE = -1e30
HIGHEST = lax.Precision.HIGHEST


def scaled_rms(values, gain):
    return values * lax.rsqrt(jnp.mean(values * values, axis=-1, keepdims=True) + 1e-06) * gain


def rotate(values, positions):
    halfway = values.shape[-1] // 2
    frequency = ROPE_BASE ** (-(jnp.arange(halfway, dtype=jnp.float32) * 2.0) / values.shape[-1])
    angles = positions.astype(jnp.float32)[..., None, None] * frequency
    cosine = jnp.cos(angles)
    sine_part = jnp.sin(angles)
    leading = values[..., :halfway]
    trailing = values[..., halfway:]
    return jnp.concatenate(
        [leading * cosine - trailing * sine_part, trailing * cosine + leading * sine_part], axis=-1
    )


def project(inputs, positions, norm_gain, query_gain, key_gain, w_query, key_matrix, value_matrix):
    number = inputs.shape[0]
    normed = scaled_rms(inputs.astype(jnp.float32), norm_gain).astype(jnp.bfloat16)
    query_rows = jnp.dot(normed, w_query, preferred_element_type=jnp.float32).reshape(
        number, -1, HEAD_SIZE
    )
    keys = jnp.dot(normed, key_matrix, preferred_element_type=jnp.float32).reshape(
        number, -1, HEAD_SIZE
    )
    values = jnp.dot(normed, value_matrix, preferred_element_type=jnp.float32).astype(jnp.bfloat16)
    query_rows = (
        rotate(scaled_rms(query_rows, query_gain), positions)
        .reshape(number, -1)
        .astype(jnp.bfloat16)
    )
    keys = rotate(scaled_rms(keys, key_gain), positions).reshape(number, -1).astype(jnp.bfloat16)
    return (query_rows, keys, values)


def shards(
    states,
    norm_gain,
    query_gain,
    key_gain,
    w_query,
    key_matrix,
    value_matrix,
    w_out,
    cached_key_blocks,
    cached_value_blocks,
    req_len,
    slot_request,
    slot_block,
    slot_empty,
):
    own_rows = states.shape[1]
    first_row = lax.axis_index("seq") * own_rows
    kv_heads = key_matrix.shape[1] // HEAD_SIZE
    q_heads = w_query.shape[1] // HEAD_SIZE
    head_sharing = q_heads // kv_heads
    query_width = w_query.shape[1]
    kv_width = key_matrix.shape[1]
    slot_count = cached_key_blocks.shape[0]
    block_len = cached_key_blocks.shape[1]
    requests = req_len.shape[0]
    scaling = HEAD_SIZE ** (-0.5)
    slot_len = jnp.take(req_len, slot_request)
    offsets = jnp.arange(block_len, dtype=jnp.int32)
    filled = (slot_empty[:, None] == 0) & (
        slot_block[:, None] * block_len + offsets[None, :] < slot_len[:, None]
    )
    filled_wide = filled[None, :, None, None, :]
    belongs = (slot_request[None, :] == jnp.arange(requests, dtype=jnp.int32)[:, None]) & (
        slot_empty[None, :] == 0
    )
    belongs_float = belongs.astype(jnp.float32)
    keys_split = cached_key_blocks.reshape(slot_count, block_len, kv_heads, HEAD_SIZE)
    values_split = cached_value_blocks.reshape(slot_count, block_len, kv_heads, HEAD_SIZE)
    turn_spans = [(sequence_index, sequence_index + 1) for sequence_index in range(STEPS)]
    past_keys = []
    past_values = []
    results = []
    for low_turn, high_turn in turn_spans:
        number = high_turn - low_turn
        turn_ids = jnp.arange(low_turn, high_turn, dtype=jnp.int32)
        block_states = states[low_turn:high_turn]
        wide_states = lax.all_gather(block_states, "mp", axis=2, tiled=True)
        portion = lax.all_gather(wide_states, "seq", axis=1, tiled=True)
        portion_rows = portion.shape[1]
        portion_positions = req_len[None, :] + turn_ids[:, None]
        part_query, part_key, part_value = project(
            portion.reshape(number * portion_rows, -1),
            portion_positions.reshape(-1),
            norm_gain,
            query_gain,
            key_gain,
            w_query,
            key_matrix,
            value_matrix,
        )
        everyone = jnp.concatenate([part_query, part_key, part_value], axis=1).reshape(
            number, portion_rows, -1
        )
        own_packed = lax.dynamic_slice_in_dim(everyone, first_row, own_rows, 1)
        all_query = everyone[:, :, :query_width]
        own_heads = own_packed[:, :, :query_width].reshape(
            number, own_rows, kv_heads, head_sharing, HEAD_SIZE
        )
        past_keys.append(own_packed[:, :, query_width : query_width + kv_width])
        past_values.append(own_packed[:, :, query_width + kv_width :])
        slot_query = jnp.take(all_query, slot_request, axis=1).reshape(
            number, slot_count, kv_heads, head_sharing, HEAD_SIZE
        )
        scores = (
            jnp.einsum(
                "tsngd,sknd->tsngk", slot_query, keys_split, preferred_element_type=jnp.float32
            )
            * scaling
        )
        slot_maximum = jnp.max(jnp.where(filled_wide, scores, NEGATIVE), axis=-1)
        row_top = jnp.max(
            jnp.where(belongs[None, :, :, None, None], slot_maximum[:, None], NEGATIVE), axis=2
        )
        slot_reference = jnp.take(row_top, slot_request, axis=1)
        weights = jnp.where(
            filled_wide,
            jnp.exp(jnp.where(filled_wide, scores - slot_reference[..., None], 0.0)),
            0.0,
        )
        slot_total = jnp.sum(weights, axis=-1)
        slot_mix = jnp.einsum(
            "tsngk,sknd->tsngd",
            weights.astype(jnp.bfloat16),
            values_split,
            preferred_element_type=jnp.float32,
        )
        row_total = jnp.einsum("bs,tsng->tbng", belongs_float, slot_total, precision=HIGHEST)
        row_mix = jnp.einsum("bs,tsngd->tbngd", belongs_float, slot_mix, precision=HIGHEST)
        every_top = lax.pmax(row_top, "seq")
        every_factor = jnp.exp(row_top - every_top)
        summed_total, summed_mix = lax.psum(
            (row_total * every_factor, row_mix * every_factor[..., None]), "seq"
        )
        own_top = lax.dynamic_slice_in_dim(every_top, first_row, own_rows, 1)
        own_total = lax.dynamic_slice_in_dim(summed_total, first_row, own_rows, 1)
        own_mix = lax.dynamic_slice_in_dim(summed_mix, first_row, own_rows, 1)
        earlier_keys = jnp.concatenate(past_keys, axis=0).reshape(
            high_turn, own_rows, kv_heads, HEAD_SIZE
        )
        earlier_values = jnp.concatenate(past_values, axis=0).reshape(
            high_turn, own_rows, kv_heads, HEAD_SIZE
        )
        fresh_scores = (
            jnp.einsum(
                "trngd,jrnd->trngj", own_heads, earlier_keys, preferred_element_type=jnp.float32
            )
            * scaling
        )
        allowed = (jnp.arange(high_turn, dtype=jnp.int32)[None, :] <= turn_ids[:, None])[
            :, None, None, None, :
        ]
        fresh_top = jnp.max(jnp.where(allowed, fresh_scores, NEGATIVE), axis=-1)
        overall = jnp.maximum(own_top, fresh_top)
        retained = jnp.exp(own_top - overall)
        fresh_weights = jnp.where(
            allowed, jnp.exp(jnp.where(allowed, fresh_scores - overall[..., None], 0.0)), 0.0
        )
        denominator = own_total * retained + jnp.sum(fresh_weights, axis=-1)
        mixture = own_mix * retained[..., None] + jnp.einsum(
            "trngj,jrnd->trngd",
            fresh_weights.astype(jnp.bfloat16),
            earlier_values,
            preferred_element_type=jnp.float32,
        )
        attended = (
            (mixture / denominator[..., None])
            .astype(jnp.bfloat16)
            .reshape(number * own_rows, query_width)
        )
        projected_out = jnp.dot(attended, w_out, preferred_element_type=jnp.float32).reshape(
            number, own_rows, -1
        )
        summed = lax.psum_scatter(projected_out, "mp", scatter_dimension=2, tiled=True)
        results.append((block_states.astype(jnp.float32) + summed).astype(jnp.bfloat16))
    return (
        jnp.concatenate(results, axis=0),
        jnp.concatenate(past_keys, axis=0),
        jnp.concatenate(past_values, axis=0),
    )


def solution(mesh):
    placed = (
        P(None, "seq", "mp"),
        P(),
        P(),
        P(),
        P(None, "mp"),
        P(None, "mp"),
        P(None, "mp"),
        P("mp", None),
        P("seq", None, "mp"),
        P("seq", None, "mp"),
        P(),
        P("seq"),
        P("seq"),
        P("seq"),
    )
    return jax.shard_map(
        shards,
        mesh=mesh,
        in_specs=placed,
        out_specs=(P(None, "seq", "mp"), P(None, "seq", "mp"), P(None, "seq", "mp")),
        check_vma=False,
    )
```

profile of v0, /device:TPU:2, one launch (start us, length us, event | category | flops | bytes accessed | tf_op | source)
XLA Modules:
  0.0 764.8 jit_solution(867895954115995821)
XLA Ops:
  8.8 12.3 %all_gather.28 = bf16[1,2,2560]{2,0,1:T(2,128)(2,1)S(1)} all-gather(bf16[1,2,640]{2,0,1:T(2,128)(2,1)S(1)} %copy.475), channel_id=1, replica_groups=mesh['seq'=64,'mp'=4] {'mp'}, dimensions={2}, use_global_device_ids=true | all-gather | bytes 12800 | tf_op jit(solution)/shard_map/all_gather | solution.py:96
  21.1 11.8 %all_gather.24 = bf16[1,2,2560]{2,0,1:T(2,128)(2,1)S(1)} all-gather(bf16[1,2,640]{2,0,1:T(2,128)(2,1)S(1)} %copy.469), channel_id=1, replica_groups=mesh['seq'=64,'mp'=4] {'mp'}, dimensions={2}, use_global_device_ids=true | all-gather | bytes 12800 | tf_op jit(solution)/shard_map/all_gather | solution.py:96
  32.9 53.2 %all_gather.25 = bf16[1,128,2560]{2,0,1:T(2,128)(2,1)S(1)} all-gather(bf16[1,2,2560]{2,0,1:T(2,128)(2,1)S(1)} %all_gather.24), channel_id=1, replica_groups=mesh['seq'=64,'mp'=4] {'seq'}, dimensions={1}, use_global_device_ids=true | all-gather | bytes 665600 | tf_op jit(solution)/shard_map/all_gather | solution.py:97
  90.1 1.6 multiply_reduce_fusion.7
  91.7 48.7 %all_gather.29 = bf16[1,128,2560]{2,0,1:T(2,128)(2,1)S(1)} all-gather(bf16[1,2,2560]{2,0,1:T(2,128)(2,1)S(1)} %all_gather.28), channel_id=1, replica_groups=mesh['seq'=64,'mp'=4] {'seq'}, dimensions={1}, use_global_device_ids=true | all-gather | bytes 665600 | tf_op jit(solution)/shard_map/all_gather | solution.py:97
  141.7 1.6 multiply_reduce_fusion.5
  143.3 11.8 %all_gather.26 = bf16[1,2,2560]{2,0,1:T(2,128)(2,1)S(1)} all-gather(bf16[1,2,640]{2,0,1:T(2,128)(2,1)S(1)} %copy.472), channel_id=1, replica_groups=mesh['seq'=64,'mp'=4] {'mp'}, dimensions={2}, use_global_device_ids=true | all-gather | bytes 12800 | tf_op jit(solution)/shard_map/all_gather | solution.py:96
  155.1 49.3 %all_gather.27 = bf16[1,128,2560]{2,0,1:T(2,128)(2,1)S(1)} all-gather(bf16[1,2,2560]{2,0,1:T(2,128)(2,1)S(1)} %all_gather.26), channel_id=1, replica_groups=mesh['seq'=64,'mp'=4] {'seq'}, dimensions={1}, use_global_device_ids=true | all-gather | bytes 665600 | tf_op jit(solution)/shard_map/all_gather | solution.py:97
  205.7 1.7 multiply_reduce_fusion.6
  207.4 11.8 %all_gather.30 = bf16[1,2,2560]{2,0,1:T(2,128)(2,1)S(1)} all-gather(bf16[1,2,640]{2,0,1:T(2,128)(2,1)S(1)} %copy.478), channel_id=1, replica_groups=mesh['seq'=64,'mp'=4] {'mp'}, dimensions={2}, use_global_device_ids=true | all-gather | bytes 12800 | tf_op jit(solution)/shard_map/all_gather | solution.py:96
  219.3 48.6 %all_gather.31 = bf16[1,128,2560]{2,0,1:T(2,128)(2,1)S(1)} all-gather(bf16[1,2,2560]{2,0,1:T(2,128)(2,1)S(1)} %all_gather.30), channel_id=1, replica_groups=mesh['seq'=64,'mp'=4] {'seq'}, dimensions={1}, use_global_device_ids=true | all-gather | bytes 665600 | tf_op jit(solution)/shard_map/all_gather | solution.py:97
  269.2 1.6 multiply_reduce_fusion.4
  270.8 4.4 copy.463
  275.3 3.8 multiply_reduce_fusion.3
  279.1 2.2 multiply_reduce_fusion
  281.3 2.2 multiply_reduce_fusion.1
  283.7 1.6 multiply_reduce_fusion.2
  295.6 2.0 multiply_multiply_fusion.3
  306.6 1.7 fusion.29
  308.3 1.6 fusion.30
  312.0 109.9 %all-reduce.2 = (f32[1,128,1,4]{1,3,2,0:T(4,128)}, f32[1,128,1,4]{1,3,2,0:T(4,128)}, f32[1,128,1,4]{1,3,2,0:T(4,128)}, f32[1,128,1,4]{1,3,2,0:T(4,128)}) all-reduce(f32[1,128,1,4]{1,3,2,0:T(4,128)} %bitcast.554, f32[1,128,1,4]{1,3,2,0:T(4,128)S(1)} %bitcast.553, ...), channel_id=1, replica_groups=mesh['seq'=64,'mp'=4] {'seq'}, use_global_device_ids=true, to_apply=%region_39.42 | all-reduce | flops 2048 | bytes 16384 | tf_op jit(solution)/shard_map/pmax | solution.py:148
  431.2 1.6 fusion.111
  445.7 111.5 %all-reduce = (f32[1,128,1,4]{1,3,2,0:T(4,128)S(1)}, f32[1,128,1,4]{1,3,2,0:T(4,128)S(1)}, f32[1,128,1,4]{1,3,2,0:T(4,128)S(1)}, f32[1,128,1,4]{1,3,2,0:T(4,128)S(1)}) all-reduce(f32[1,128,1,4]{1,3,2,0:T(4,128)S(1)} %fusion.33, f32[1,128,1,4]{1,3,2,0:T(4,128)S(1)} %fusion.34, ...), channel_id=1, replica_groups=mesh['seq'=64,'mp'=4] {'seq'}, use_global_device_ids=true, to_apply=%region_43.46 | all-reduce | flops 2048 | bytes 16384 | tf_op jit(solution)/shard_map/psum | solution.py:150
  559.7 80.1 %all-reduce.5.cloned.1.call-done = (f32[1,128,1,4,128]{1,4,3,2,0:T(8,128)}, f32[1,128,1,4,128]{1,4,3,2,0:T(8,128)}, f32[1,128,1,4,128]{1,4,3,2,0:T(8,128)}, f32[1,128,1,4,128]{1,4,3,2,0:T(8,128)}) async-done(((f32[1,128,1,4,128]{1,4,3,2,0:T(8,128)}, f32[1,128,1,4,128]{1,4,3,2,0:T(8,128)}, f32[1,128,1,4,128]{1,4,3,2,0:T(8,128)}, f32[1,128,1,4,128]{1,4,3,2,0:T(8,128)}), (f32[1,128,1,4,128]{1,4,3,2,0:T(8,128)}, ...) | async-done | bytes 1048592 | tf_op jit(solution)/shard_map/psum | solution.py:150
  640.9 2.2 convolution_bitcast_fusion
  644.2 2.2 convolution_bitcast_fusion.1
  647.5 2.2 convolution_bitcast_fusion.2
  650.8 2.2 convolution_bitcast_fusion.3
  654.2 13.9 %reduce-scatter.19.cloned.1.call-done = f32[640,2]{1,0:T(8,128)} async-done(((f32[2560,2]{1,0:T(8,128)}), f32[640,2]{1,0:T(8,128)}) %reduce-scatter.19.cloned.1.call-update) | async-done | bytes 5136
  669.2 28.5 %reduce-scatter.17.cloned.1.call-done = f32[640,2]{1,0:T(8,128)} async-done(((f32[2560,2]{1,0:T(8,128)}), f32[640,2]{1,0:T(8,128)}) %reduce-scatter.17.cloned.1.call-update) | async-done | bytes 5136
  698.8 28.3 %reduce-scatter.15.cloned.1.call-done = f32[640,2]{1,0:T(8,128)} async-done(((f32[2560,2]{1,0:T(8,128)}), f32[640,2]{1,0:T(8,128)}) %reduce-scatter.15.cloned.1.call-update) | async-done | bytes 5136
  728.2 28.3 %reduce-scatter.13.cloned.1.call-done = f32[640,2]{1,0:T(8,128)} async-done(((f32[2560,2]{1,0:T(8,128)}), f32[640,2]{1,0:T(8,128)}) %reduce-scatter.13.cloned.1.call-update) | async-done | bytes 5136
  (365 shorter events, 65.3 us)
Async XLA Ops:
  7.2 633.7 %copy-start = (bf16[512,2560]{1,0:T(8,128)(2,1)S(1)}, bf16[512,2560]{1,0:T(8,128)(2,1)}, u32[]{:S(2)}) copy-start(bf16[512,2560]{1,0:T(8,128)(2,1)} %param.25) | copy-start | bytes 7864324
  7.2 632.6 %all-reduce.5.cloned.1.call-start = ((), (), s32[]{:S(2)}) async-start(), calls=%async_computation.8 | async-start | bytes 2097152 | tf_op jit(solution)/shard_map/psum | solution.py:150
  8.7 24.2 %copy-start.34 = (bf16[1,2,640]{2,1,0:T(2,128)(2,1)}, bf16[1,2,640]{2,1,0:T(2,128)(2,1)S(1)}, u32[]{:S(2)}) copy-start(bf16[1,2,640]{2,1,0:T(2,128)(2,1)S(1)} %get-tuple-element.84) | copy-start | bytes 7684
  8.7 24.2 %copy-start.38 = (bf16[1,2,640]{2,1,0:T(2,128)(2,1)}, bf16[1,2,640]{2,1,0:T(2,128)(2,1)S(1)}, u32[]{:S(2)}) copy-start(bf16[1,2,640]{2,1,0:T(2,128)(2,1)S(1)} %get-tuple-element.85) | copy-start | bytes 7684
  8.7 134.6 %copy-start.36 = (bf16[1,2,640]{2,1,0:T(2,128)(2,1)}, bf16[1,2,640]{2,1,0:T(2,128)(2,1)S(1)}, u32[]{:S(2)}) copy-start(bf16[1,2,640]{2,1,0:T(2,128)(2,1)S(1)} %get-tuple-element.86) | copy-start | bytes 7684
  8.7 198.7 %copy-start.40 = (bf16[1,2,640]{2,1,0:T(2,128)(2,1)}, bf16[1,2,640]{2,1,0:T(2,128)(2,1)S(1)}, u32[]{:S(2)}) copy-start(bf16[1,2,640]{2,1,0:T(2,128)(2,1)S(1)} %get-tuple-element.87) | copy-start | bytes 7684
  283.6 7.1 copy-start.69
  283.6 7.1 copy-start.12
  283.6 7.1 copy-start.22
  283.6 7.1 copy-start.23
  283.6 7.1 copy-start.24
  283.6 7.1 copy-start.62
  285.3 10.3 %copy-start.60 = (f32[128,4]{0,1:T(4,128)S(1)}, f32[128,4]{0,1:T(4,128)}, u32[]{:S(2)}) copy-start(f32[128,4]{0,1:T(4,128)} %get-tuple-element.150) | copy-start | bytes 6148
  285.3 10.3 %copy-start.59 = (f32[128,4]{0,1:T(4,128)S(1)}, f32[128,4]{0,1:T(4,128)}, u32[]{:S(2)}) copy-start(f32[128,4]{0,1:T(4,128)} %get-tuple-element.152) | copy-start | bytes 6148
  285.3 10.3 %copy-start.55 = (f32[128,4]{0,1:T(4,128)S(1)}, f32[128,4]{0,1:T(4,128)}, u32[]{:S(2)}) copy-start(f32[128,4]{0,1:T(4,128)} %get-tuple-element.146) | copy-start | bytes 6148
  285.3 25.0 %copy-start.45 = (pred[16]{0:T(512)(128)(4,1)}, pred[16]{0:T(512)(128)(4,1)S(1)}, u32[]{:S(2)}) copy-start(pred[16]{0:T(512)(128)(4,1)S(1)} %broadcast_compare_fusion) | copy-start | bytes 52
  286.5 19.3 %copy-start.42 = (s32[1024]{0:T(1024)}, s32[1024]{0:T(1024)S(1)}, u32[]{:S(2)}) copy-start(s32[1024]{0:T(1024)S(1)} %pad_clamp_fusion) | copy-start | bytes 12292
  287.7 18.7 %copy-start.58 = (pred[16]{0:T(512)(128)(4,1)}, pred[16]{0:T(512)(128)(4,1)S(1)}, u32[]{:S(2)}) copy-start(pred[16]{0:T(512)(128)(4,1)S(1)} %get-tuple-element.53) | copy-start | bytes 52
  311.4 114.5 %copy-start.25 = (f32[128,4]{0,1:T(4,128)}, f32[128,4]{0,1:T(4,128)S(1)}, u32[]{:S(2)}) copy-start(f32[128,4]{0,1:T(4,128)S(1)} %get-tuple-element.28) | copy-start | bytes 6148
  311.4 114.5 %copy-start.27 = (f32[128,4]{0,1:T(4,128)}, f32[128,4]{0,1:T(4,128)S(1)}, u32[]{:S(2)}) copy-start(f32[128,4]{0,1:T(4,128)S(1)} %get-tuple-element.31) | copy-start | bytes 6148
  436.2 6.8 copy-start.49
  437.3 6.7 copy-start.47
  437.3 7.2 copy-start.50
  438.5 6.8 copy-start.26
  439.6 228.5 %reduce-scatter.19.cloned.1.call-start = ((), (), s32[]{:S(2)}) async-start(), calls=%async_computation.7 | async-start | bytes 1638400
  643.1 54.5 %reduce-scatter.17.cloned.1.call-start = ((), (), s32[]{:S(2)}) async-start(), calls=%async_computation.6 | async-start | bytes 1638400
  646.4 80.6 %reduce-scatter.15.cloned.1.call-start = ((), (), s32[]{:S(2)}) async-start(), calls=%async_computation.5 | async-start | bytes 1638400
  649.7 106.7 %reduce-scatter.13.cloned.1.call-start = ((), (), s32[]{:S(2)}) async-start(), calls=%async_computation.4 | async-start | bytes 1638400
  653.0 104.5 %copy-start.39 = (bf16[1,2,640]{2,1,0:T(2,128)(2,1)S(1)}, bf16[1,2,640]{2,1,0:T(2,128)(2,1)}, u32[]{:S(2)}) copy-start(bf16[1,2,640]{2,1,0:T(2,128)(2,1)} %copy-done.38) | copy-start | bytes 7684
  653.0 104.5 %copy-start.41 = (bf16[1,2,640]{2,1,0:T(2,128)(2,1)S(1)}, bf16[1,2,640]{2,1,0:T(2,128)(2,1)}, u32[]{:S(2)}) copy-start(bf16[1,2,640]{2,1,0:T(2,128)(2,1)} %copy-done.40) | copy-start | bytes 7684
  653.0 104.6 %copy-start.35 = (bf16[1,2,640]{2,1,0:T(2,128)(2,1)S(1)}, bf16[1,2,640]{2,1,0:T(2,128)(2,1)}, u32[]{:S(2)}) copy-start(bf16[1,2,640]{2,1,0:T(2,128)(2,1)} %copy-done.34) | copy-start | bytes 7684
  653.0 104.6 %copy-start.37 = (bf16[1,2,640]{2,1,0:T(2,128)(2,1)S(1)}, bf16[1,2,640]{2,1,0:T(2,128)(2,1)}, u32[]{:S(2)}) copy-start(bf16[1,2,640]{2,1,0:T(2,128)(2,1)} %copy-done.36) | copy-start | bytes 7684
  (49 other events, 153.2 us)
Sparse Core Ops, SparseCore 0:
  439.8 199.9 all-reduce.4
  643.3 24.8 reduce-scatter.18
  670.8 26.7 reduce-scatter.16
  700.2 26.7 reduce-scatter.14
  729.6 26.7 reduce-scatter.12
where the time goes:
time: 766 us; the launch traced here: 765 us
  blocking collectives  469 us (61%)
  waiting for transfers between devices  179 us (23%)
  matrix products  43.9 us (6%)
  local copies, waits for them, and re-layouts  32.9 us (4%)
  other arithmetic  24.7 us (3%)
  between operations  14.9 us (2%)
    all_gather x4, blocking collectives, shards(): portion = lax.all_gather(wide_states, 'seq', axis=1, tiled=True)  200 us
    psum x1, blocking collectives, shards(): lax.psum((row_total * every_factor, row_mix * every_factor[..., None]), '...  112 us
    pmax x1, blocking collectives, shards(): every_top = lax.pmax(row_top, 'seq')  110 us
    unnamed x9, waiting for transfers between devices  99 us
    psum x1, waiting for transfers between devices, shards(): lax.psum((row_total * every_factor, row_mix * every_factor[..., None]), '...  80.1 us
    all_gather x4, blocking collectives, shards(): wide_states = lax.all_gather(block_states, 'mp', axis=2, tiled=True)  47.8 us
  transfers between devices with their start and end apart: 5, of which 5 were waited for; matrix products, arithmetic and copies ran while one was open for 3% of the time, Pallas kernels for 0%

commit v1 on v0

--- a/solution.py
+++ b/solution.py
@@ -94,7 +94,10 @@
         turn_ids = jnp.arange(low_turn, high_turn, dtype=jnp.int32)
         block_states = states[low_turn:high_turn]
         wide_states = lax.all_gather(block_states, "mp", axis=2, tiled=True)
-        portion = lax.all_gather(wide_states, "seq", axis=1, tiled=True)
+        size = lax.axis_size("seq")
+        tiles = jnp.stack([wide_states for _ in range(size)])
+        tiles = lax.all_to_all(tiles, "seq", split_axis=0, concat_axis=0)
+        portion = jnp.concatenate(tiles, axis=1)
         portion_rows = portion.shape[1]
         portion_positions = req_len[None, :] + turn_ids[:, None]
         part_query, part_key, part_value = project(

time: 766 us -> 802 us (1.047); the launches traced: 765 us -> 793 us
  blocking collectives: 469 us -> 270 us
  waiting for transfers between devices: 179 us -> 322 us
  starting transfers between devices: 0.21 us -> 38 us
  local copies, waits for them, and re-layouts: 32.9 us -> 65.9 us
  other arithmetic: 24.7 us -> 39.1 us
    all_gather x4 -> x0, blocking collectives: 200 us -> none  [shards(): portion = lax.all_gather(wide_states, 'seq', axis=1, tiled=True)]
    psum x1, waiting for transfers between devices: 80.1 us -> 211 us  [shards(): lax.psum((row_total * every_factor, row_mix * every_factor[..., None]), '...]
    all_to_all x0 -> x4, starting transfers between devices: none -> 37.1 us  [shards(): tiles = lax.all_to_all(tiles, 'seq', split_axis=0, concat_axis=0)]
    convert_element_type x0 -> x8, local copies, waits for them, and re-layouts: none -> 20.9 us  [the longest x4 11.5 us: project(): inputs.astype(jnp.float32)]
    all_to_all x0 -> x4, waiting for transfers between devices: none -> 12.2 us  [shards(): tiles = lax.all_to_all(tiles, 'seq', split_axis=0, concat_axis=0)]
  transfers between devices with their start and end apart: 5 -> 9, of which waited for: 5 -> 7; matrix products, arithmetic and copies ran while one was open for 3% -> 6% of each run, Pallas kernels for 0% -> 0%
where the time goes in v1:
time: 802 us; the launch traced here: 793 us
  waiting for transfers between devices  322 us (40%)
  blocking collectives  270 us (34%)
  local copies, waits for them, and re-layouts  65.9 us (8%)
  matrix products  43 us (5%)
  other arithmetic  39.1 us (5%)
  starting transfers between devices  38 us (5%)
  between operations  15.2 us (2%)
    psum x1, waiting for transfers between devices, shards(): lax.psum((row_total * every_factor, row_mix * every_factor[..., None]), '...  211 us
    psum x1, blocking collectives, shards(): lax.psum((row_total * every_factor, row_mix * every_factor[..., None]), '...  113 us
    pmax x1, blocking collectives, shards(): every_top = lax.pmax(row_top, 'seq')  109 us
    unnamed x9, waiting for transfers between devices  98.4 us
    all_gather x4, blocking collectives, shards(): wide_states = lax.all_gather(block_states, 'mp', axis=2, tiled=True)  47.7 us
    all_to_all x4, starting transfers between devices, shards(): tiles = lax.all_to_all(tiles, 'seq', split_axis=0, concat_axis=0)  37.1 us
  transfers between devices with their start and end apart: 9, of which 7 were waited for; matrix products, arithmetic and copies ran while one was open for 6% of the time, Pallas kernels for 0%

profile of v1, /device:TPU:2, one launch (start us, length us, event | category | flops | bytes accessed | tf_op | source)
XLA Modules:
  0.0 792.6 jit_solution(7862718056658459816)
XLA Ops:
  8.1 12.3 %all_gather.26 = bf16[1,2,2560]{2,1,0:T(2,128)(2,1)S(1)} all-gather(bf16[1,2,640]{2,1,0:T(2,128)(2,1)S(1)} %get-tuple-element.88), channel_id=1, replica_groups=mesh['seq'=64,'mp'=4] {'mp'}, dimensions={2}, use_global_device_ids=true | all-gather | bytes 12800 | tf_op jit(solution)/shard_map/all_gather | solution.py:96
  21.6 12.0 %all-to-all-start.3 = ((bf16[64,1,2,2560]{3,2,1,0:T(2,128)(2,1)}), bf16[64,1,2,2560]{3,2,1,0:T(2,128)(2,1)S(1)}, u32[]{:S(2)}, u32[]{:S(2)}) async-start(bf16[64,1,2,2560]{3,2,1,0:T(2,128)(2,1)} %stack.11), calls=%async_computation.3 | async-start | bytes 1310720 | tf_op jit(solution)/shard_map/all_to_all | solution.py:99
  33.6 11.9 %all_gather.22 = bf16[1,2,2560]{2,1,0:T(2,128)(2,1)S(1)} all-gather(bf16[1,2,640]{2,1,0:T(2,128)(2,1)S(1)} %get-tuple-element.87), channel_id=1, replica_groups=mesh['seq'=64,'mp'=4] {'mp'}, dimensions={2}, use_global_device_ids=true | all-gather | bytes 12800 | tf_op jit(solution)/shard_map/all_gather | solution.py:96
  45.6 7.3 all-to-all-done.3
  54.0 7.3 all-to-all-start.1
  62.0 11.8 %all_gather.20 = bf16[1,2,2560]{2,1,0:T(2,128)(2,1)S(1)} all-gather(bf16[1,2,640]{2,1,0:T(2,128)(2,1)S(1)} %get-tuple-element.86), channel_id=1, replica_groups=mesh['seq'=64,'mp'=4] {'mp'}, dimensions={2}, use_global_device_ids=true | all-gather | bytes 12800 | tf_op jit(solution)/shard_map/all_gather | solution.py:96
  75.7 4.9 all-to-all-done.1
  81.7 7.3 all-to-all-start
  89.5 4.4 copy.424
  93.9 11.8 %all_gather.24 = bf16[1,2,2560]{2,1,0:T(2,128)(2,1)S(1)} all-gather(bf16[1,2,640]{2,1,0:T(2,128)(2,1)S(1)} %get-tuple-element.89), channel_id=1, replica_groups=mesh['seq'=64,'mp'=4] {'mp'}, dimensions={2}, use_global_device_ids=true | all-gather | bytes 12800 | tf_op jit(solution)/shard_map/all_gather | solution.py:96
  111.5 10.5 %all-to-all-start.2 = ((bf16[64,1,2,2560]{3,2,1,0:T(2,128)(2,1)}), bf16[64,1,2,2560]{3,2,1,0:T(2,128)(2,1)}, u32[]{:S(2)}, u32[]{:S(2)}) async-start(bf16[64,1,2,2560]{3,2,1,0:T(2,128)(2,1)} %stack.10), calls=%async_computation.2 | async-start | bytes 1310720 | tf_op jit(solution)/shard_map/all_to_all | solution.py:99
  124.5 2.9 reshape.1255
  127.4 2.3 convolution_convert_fusion.3
  129.8 2.9 reshape.1257
  132.6 2.9 reshape.1259
  135.6 2.5 convolution_convert_fusion.2
  146.0 2.9 reshape.1258
  148.8 2.6 convolution_convert_fusion.1
  153.0 5.2 multiply_convert_fusion.7
  158.2 2.7 reshape.1405
  167.6 2.9 reshape.1409
  170.5 2.7 reshape.1410
  174.3 2.9 multiply_reduce_fusion.4
  218.6 109.1 %all-reduce.2 = (f32[1,128,1,4]{1,3,2,0:T(4,128)S(1)}, f32[1,128,1,4]{1,3,2,0:T(4,128)S(1)}, f32[1,128,1,4]{1,3,2,0:T(4,128)S(1)}, f32[1,128,1,4]{1,3,2,0:T(4,128)S(1)}) all-reduce(f32[1,128,1,4]{1,3,2,0:T(4,128)S(1)} %bitcast.481, f32[1,128,1,4]{1,3,2,0:T(4,128)S(1)} %bitcast.480, ...), channel_id=1, replica_groups=mesh['seq'=64,'mp'=4] {'seq'}, use_global_device_ids=true, to_apply=%region_39.42 | all-reduce | flops 2048 | bytes 16384 | tf_op jit(solution)/shard_map/pmax | solution.py:151
  334.2 112.8 %all-reduce = (f32[1,128,1,4]{1,3,2,0:T(4,128)}, f32[1,128,1,4]{1,3,2,0:T(4,128)}, f32[1,128,1,4]{1,3,2,0:T(4,128)S(1)}, f32[1,128,1,4]{1,3,2,0:T(4,128)S(1)}) all-reduce(f32[1,128,1,4]{1,3,2,0:T(4,128)S(1)} %fusion.9, f32[1,128,1,4]{1,3,2,0:T(4,128)S(1)} %fusion.10, ...), channel_id=1, replica_groups=mesh['seq'=64,'mp'=4] {'seq'}, use_global_device_ids=true, to_apply=%region_43.46 | all-reduce | flops 2048 | bytes 16384 | tf_op jit(solution)/shard_map/psum | solution.py:153
  456.0 211.4 %all-reduce.5.cloned.1.call-done = (f32[1,128,1,4,128]{1,4,3,2,0:T(8,128)}, f32[1,128,1,4,128]{1,4,3,2,0:T(8,128)}, f32[1,128,1,4,128]{1,4,3,2,0:T(8,128)}, f32[1,128,1,4,128]{1,4,3,2,0:T(8,128)}) async-done(((f32[1,128,1,4,128]{1,4,3,2,0:T(8,128)}, f32[1,128,1,4,128]{1,4,3,2,0:T(8,128)}, f32[1,128,1,4,128]{1,4,3,2,0:T(8,128)}, f32[1,128,1,4,128]{1,4,3,2,0:T(8,128)}), (f32[1,128,1,4,128]{1,4,3,2,0:T(8,128)}, ...) | async-done | bytes 1048592 | tf_op jit(solution)/shard_map/psum | solution.py:153
  668.5 2.2 convolution_bitcast_fusion
  678.5 2.2 convolution_bitcast_fusion.3
  682.6 13.2 %reduce-scatter.19.cloned.1.call-done = f32[640,2]{1,0:T(8,128)} async-done(((f32[2560,2]{1,0:T(8,128)}), f32[640,2]{1,0:T(8,128)}) %reduce-scatter.19.cloned.1.call-update) | async-done | bytes 5136
  696.9 28.5 %reduce-scatter.17.cloned.1.call-done = f32[640,2]{1,0:T(8,128)} async-done(((f32[2560,2]{1,0:T(8,128)}), f32[640,2]{1,0:T(8,128)}) %reduce-scatter.17.cloned.1.call-update) | async-done | bytes 5136
  726.4 28.3 %reduce-scatter.15.cloned.1.call-done = f32[640,2]{1,0:T(8,128)} async-done(((f32[2560,2]{1,0:T(8,128)}), f32[640,2]{1,0:T(8,128)}) %reduce-scatter.15.cloned.1.call-update) | async-done | bytes 5136
  755.8 28.3 %reduce-scatter.13.cloned.1.call-done = f32[640,2]{1,0:T(8,128)} async-done(((f32[2560,2]{1,0:T(8,128)}), f32[640,2]{1,0:T(8,128)}) %reduce-scatter.13.cloned.1.call-update) | async-done | bytes 5136
  (388 shorter events, 104.7 us)
Async XLA Ops:
  7.2 661.3 %copy-start = (bf16[512,2560]{1,0:T(8,128)(2,1)S(1)}, bf16[512,2560]{1,0:T(8,128)(2,1)}, u32[]{:S(2)}) copy-start(bf16[512,2560]{1,0:T(8,128)(2,1)} %param.25) | copy-start | bytes 7864324
  7.2 38.3 %copy-start.32 = (s32[16]{0:T(128)S(1)}, s32[16]{0:T(128)}, u32[]{:S(2)}) copy-start(s32[16]{0:T(128)} %param.29) | copy-start | bytes 196
  21.6 31.3 %all-to-all-start.3 = ((bf16[64,1,2,2560]{3,2,1,0:T(2,128)(2,1)}), bf16[64,1,2,2560]{3,2,1,0:T(2,128)(2,1)S(1)}, u32[]{:S(2)}, u32[]{:S(2)}) async-start(bf16[64,1,2,2560]{3,2,1,0:T(2,128)(2,1)} %stack.11), calls=%async_computation.3 | async-start | bytes 1310720 | tf_op jit(solution)/shard_map/all_to_all | solution.py:99
  33.6 27.8 %copy-start.1 = (s32[128]{0:T(128)S(1)}, s32[128]{0:T(128)}, u32[]{:S(2)}) copy-start(s32[128]{0:T(128)} %param.28) | copy-start | bytes 1540
  33.6 40.7 %copy-start.80 = (s32[16]{0:T(128)S(1)}, s32[16]{0:T(128)}, u32[]{:S(2)}) copy-start(s32[16]{0:T(128)} %param.31) | copy-start | bytes 196
  33.6 41.4 %copy-start.71 = (s32[16]{0:T(128)S(1)}, s32[16]{0:T(128)}, u32[]{:S(2)}) copy-start(s32[16]{0:T(128)} %param.30) | copy-start | bytes 196
  45.5 36.2 %copy-start.30 = (s32[1024]{0:T(1024)}, s32[1024]{0:T(1024)S(1)}, u32[]{:S(2)}) copy-start(s32[1024]{0:T(1024)S(1)} %pad_clamp_fusion) | copy-start | bytes 12292
  52.8 54.5 %copy-start.12 = (bf16[64,1,2,2560]{3,2,1,0:T(2,128)(2,1)}, bf16[64,1,2,2560]{3,2,1,0:T(2,128)(2,1)S(1)}, u32[]{:S(2)}) copy-start(bf16[64,1,2,2560]{3,2,1,0:T(2,128)(2,1)S(1)} %all-to-all-done.3) | copy-start | bytes 1966084
  54.0 26.5 %all-to-all-start.1 = ((bf16[64,1,2,2560]{3,2,1,0:T(2,128)(2,1)}), bf16[64,1,2,2560]{3,2,1,0:T(2,128)(2,1)}, u32[]{:S(2)}, u32[]{:S(2)}) async-start(bf16[64,1,2,2560]{3,2,1,0:T(2,128)(2,1)} %stack.9), calls=%async_computation.1 | async-start | bytes 1310720 | tf_op jit(solution)/shard_map/all_to_all | solution.py:99
  61.4 44.8 %copy-start.52 = (f32[64]{0:T(128)}, f32[64]{0:T(128)S(1)}, u32[]{:S(2)}) copy-start(f32[64]{0:T(128)S(1)} %multiply_power_fusion) | copy-start | bytes 772
  74.3 19.6 %copy-start.34 = (pred[16]{0:T(512)(128)(4,1)}, pred[16]{0:T(512)(128)(4,1)S(1)}, u32[]{:S(2)}) copy-start(pred[16]{0:T(512)(128)(4,1)S(1)} %broadcast_compare_fusion) | copy-start | bytes 52
  74.4 31.8 %copy-start.59 = (f32[128]{0:T(128)}, f32[128]{0:T(128)S(1)}, u32[]{:S(2)}) copy-start(f32[128]{0:T(128)S(1)} %get-tuple-element.133) | copy-start | bytes 1540
  74.4 31.8 %copy-start.60 = (f32[128]{0:T(128)}, f32[128]{0:T(128)S(1)}, u32[]{:S(2)}) copy-start(f32[128]{0:T(128)S(1)} %get-tuple-element.132) | copy-start | bytes 1540
  74.4 31.8 %copy-start.62 = (f32[128]{0:T(128)}, f32[128]{0:T(128)S(1)}, u32[]{:S(2)}) copy-start(f32[128]{0:T(128)S(1)} %get-tuple-element.134) | copy-start | bytes 1540
  74.4 31.8 %copy-start.64 = (f32[128]{0:T(128)}, f32[128]{0:T(128)S(1)}, u32[]{:S(2)}) copy-start(f32[128]{0:T(128)S(1)} %get-tuple-element.135) | copy-start | bytes 1540
  81.7 28.6 %all-to-all-start = ((bf16[64,1,2,2560]{3,2,1,0:T(2,128)(2,1)}), bf16[64,1,2,2560]{3,2,1,0:T(2,128)(2,1)}, u32[]{:S(2)}, u32[]{:S(2)}) async-start(bf16[64,1,2,2560]{3,2,1,0:T(2,128)(2,1)} %stack.8), calls=%async_computation | async-start | bytes 1310720 | tf_op jit(solution)/shard_map/all_to_all | solution.py:99
  108.3 29.7 %copy-start.54 = (f32[128]{0:T(128)}, f32[128]{0:T(128)S(1)}, u32[]{:S(2)}) copy-start(f32[128]{0:T(128)S(1)} %rsqrt.126) | copy-start | bytes 1540
  110.3 25.2 %copy-start.56 = (f32[128]{0:T(128)}, f32[128]{0:T(128)S(1)}, u32[]{:S(2)}) copy-start(f32[128]{0:T(128)S(1)} %rsqrt.118) | copy-start | bytes 1540
  111.5 31.9 %all-to-all-start.2 = ((bf16[64,1,2,2560]{3,2,1,0:T(2,128)(2,1)}), bf16[64,1,2,2560]{3,2,1,0:T(2,128)(2,1)}, u32[]{:S(2)}, u32[]{:S(2)}) async-start(bf16[64,1,2,2560]{3,2,1,0:T(2,128)(2,1)} %stack.10), calls=%async_computation.2 | async-start | bytes 1310720 | tf_op jit(solution)/shard_map/all_to_all | solution.py:99
  122.0 545.4 %all-reduce.5.cloned.1.call-start = ((), (), s32[]{:S(2)}) async-start(), calls=%async_computation.12 | async-start | bytes 2097152 | tf_op jit(solution)/shard_map/psum | solution.py:153
  182.8 12.6 %copy-start.37 = (bf16[1,2,768]{2,1,0:T(2,128)(2,1)}, bf16[1,2,768]{2,1,0:T(2,128)(2,1)S(1)}, u32[]{:S(2)}) copy-start(bf16[1,2,768]{2,1,0:T(2,128)(2,1)S(1)} %fusion.90) | copy-start | bytes 9220
  189.0 11.2 %copy-start.38 = (bf16[1,2,768]{2,1,0:T(2,128)(2,1)}, bf16[1,2,768]{2,1,0:T(2,128)(2,1)S(1)}, u32[]{:S(2)}) copy-start(bf16[1,2,768]{2,1,0:T(2,128)(2,1)S(1)} %fusion.91) | copy-start | bytes 9220
  196.4 7.2 copy-start.39
  216.6 116.7 %copy-start.33 = (s32[16]{0:T(128)S(1)}, s32[16]{0:T(128)}, u32[]{:S(2)}) copy-start(s32[16]{0:T(128)} %param.29) | copy-start | bytes 196
  216.6 116.7 %copy-start.35 = (pred[16]{0:T(512)(128)(4,1)S(1)}, pred[16]{0:T(512)(128)(4,1)}, u32[]{:S(2)}) copy-start(pred[16]{0:T(512)(128)(4,1)} %copy-done.34) | copy-start | bytes 52
  332.0 120.8 %copy-start.36 = (f32[1,2,1,4]{1,3,2,0:T(4,128)}, f32[1,2,1,4]{1,3,2,0:T(4,128)S(1)}, u32[]{:S(2)}) copy-start(f32[1,2,1,4]{1,3,2,0:T(4,128)S(1)} %get-tuple-element.49) | copy-start | bytes 100
  450.5 216.9 %copy-start.43 = (f32[2,4]{0,1:T(4,128)S(1)}, f32[2,4]{0,1:T(4,128)}, u32[]{:S(2)}) copy-start(f32[2,4]{0,1:T(4,128)} %get-tuple-element.50) | copy-start | bytes 100
  452.8 243.0 %reduce-scatter.19.cloned.1.call-start = ((), (), s32[]{:S(2)}) async-start(), calls=%async_computation.11 | async-start | bytes 1638400
  670.8 54.5 %reduce-scatter.17.cloned.1.call-start = ((), (), s32[]{:S(2)}) async-start(), calls=%async_computation.10 | async-start | bytes 1638400
  674.1 80.6 %reduce-scatter.15.cloned.1.call-start = ((), (), s32[]{:S(2)}) async-start(), calls=%async_computation.9 | async-start | bytes 1638400
  677.4 106.7 %reduce-scatter.13.cloned.1.call-start = ((), (), s32[]{:S(2)}) async-start(), calls=%async_computation.8 | async-start | bytes 1638400
  680.7 104.5 %copy-start.29 = (bf16[4,2,640]{2,1,0:T(2,128)(2,1)S(1)}, bf16[4,2,640]{2,1,0:T(2,128)(2,1)}, u32[]{:S(2)}) copy-start(bf16[4,2,640]{2,1,0:T(2,128)(2,1)} %param.18) | copy-start | bytes 30724
  (62 other events, 142.1 us)
Sparse Core Ops, SparseCore 0:
  452.9 214.4 all-reduce.4
  670.9 24.8 reduce-scatter.18
  698.5 26.7 reduce-scatter.16
  727.9 26.7 reduce-scatter.14
  757.3 26.7 reduce-scatter.12
